TPU v7x, 256 devices: a whole 4x4x8 slice. The times are simulated.
256 devices in a mesh: tm: 8 (over z), space: 16 (over y, x), branch: 2 (over core).
Axes of the slice: x: 4, y: 4, z: 8, core: 2. Of those that a mesh axis runs over, the one named last changes fastest.
Arguments:
- state: float32 [2, 8, 2, 256, 1024], P('branch', 'tm', None, 'space'), may hold values from -13 to 15
- panel: float32 [2, 8, 16, 2, 256, 1024], P('branch', 'tm', None, None, 'space'), may hold values from -4 to 4
- region: int32 [256, 1024], P('space'), may hold values from 0 to 5
- feed_table: float32 [6], replicated, may hold values from 0.5 to 2.5
- step_counts: int32 [8], P('tm'), may hold values from 2 to 5, as said below
Outputs:
- deflated: float32 [2, 8, 2, 256, 1024], P('branch', 'tm', None, 'space')
- correction: float32 [2, 8, 2, 256, 1024], P('branch', 'tm', None, 'space')
- coefficients: float32 [2, 16], P('branch')
Inputs may be any that keep to these rules, and one draw needn't show every extreme that they name: `step_counts`: some segment takes 5 steps.
All inputs are finite; a program needn't handle non-finite values.
Results may differ from a plain program's by a relative error of at most 0.0003.
Values sent between devices are 32-bit elements; how exact they have to be, the bound alone decides.
No kernel may reach another device: no remote copies, remote signals or barrier semaphores. Data moves between devices by JAX's collectives and lax.ppermute only.
A program may use at most 64 MiB of HBM per device.

v0:
```python
import functools

import jax
import jax.numpy as jnp
from jax import lax
from jax.sharding import Mesh
from jax.sharding import PartitionSpec as P

STEPS = 5
SPACE = ("space_0", "space_1")
TM_SPACE = ("tm", "space_0", "space_1")


TIME_STEP = 0.03
ACTIVATOR_DIFFUSION = 1.0
INHIBITOR_DIFFUSION = 6.0
REACTION_RATE = 2.5
SMALL_EPSILON = 1e-06
HIGHEST = lax.Precision.HIGHEST


def extended_2(cells, sides, width):
    for axis, dim in sides:
        count = lax.axis_size(axis)
        head = lax.slice_in_dim(cells, 0, width, axis=dim)
        tail = lax.slice_in_dim(cells, cells.shape[dim] - width, cells.shape[dim], axis=dim)
        cells = jnp.concatenate(
            [
                lax.ppermute(tail, axis, [(i, (i + 1) % count) for i in range(count)]),
                cells,
                lax.ppermute(head, axis, [((i + 1) % count, i) for i in range(count)]),
            ],
            axis=dim,
        )
    return cells


def swapped(value, axis, apart):
    mask = 2**apart
    pairs = [(source, source ^ mask) for source in range(lax.axis_size(axis))]
    return lax.ppermute(value, axis, pairs)


def passed_along(block, axis, distance):
    devices = range(lax.axis_size(axis))
    route = [((i - distance) % len(devices), i) for i in devices]
    return lax.ppermute(block, axis, route)


def one_axis_at_a_time(x, axes):
    return functools.reduce(lax.psum, axes, x)


def laplacian_rows(extended):
    interior = extended[:, 1:-1, :]
    return (
        extended[:, 2:, :]
        + extended[:, :-2, :]
        + jnp.roll(interior, 1, 2)
        + jnp.roll(interior, -1, 2)
        - 4.0 * interior
    )


def advance(extended, feed_rate, active):
    laplacian = laplacian_rows(extended)
    interior = extended[:, 1:-1, :]
    activator = interior[0]
    inhibitor = interior[1]
    squared = activator * activator
    product = activator * inhibitor
    new_activator = activator + TIME_STEP * (
        ACTIVATOR_DIFFUSION * laplacian[0]
        + feed_rate
        - (REACTION_RATE + 1.0) * activator
        + squared * inhibitor
    )
    new_inhibitor = inhibitor + TIME_STEP * (
        INHIBITOR_DIFFUSION * laplacian[1] + REACTION_RATE * activator - squared * inhibitor
    )
    tangent_act = interior[2::2]
    tangent_inh = interior[3::2]
    new_tangent_act = tangent_act + TIME_STEP * (
        ACTIVATOR_DIFFUSION * laplacian[2::2]
        + (2.0 * product - REACTION_RATE - 1.0) * tangent_act
        + squared * tangent_inh
    )
    new_tangent_inh = tangent_inh + TIME_STEP * (
        INHIBITOR_DIFFUSION * laplacian[3::2]
        + (REACTION_RATE - 2.0 * product) * tangent_act
        - squared * tangent_inh
    )
    tangents = jnp.stack([new_tangent_act, new_tangent_inh], 1).reshape(
        tangent_act.shape[0] * 2, activator.shape[0], activator.shape[1]
    )
    advanced = jnp.concatenate([new_activator[None], new_inhibitor[None], tangents], 0)
    return jnp.where(active, advanced, interior)


def solve_small(gram, rhs):
    size = gram.shape[0]
    index = jnp.arange(size)
    columns = []
    pivots = []
    for outer in range(size):
        value = gram[:, outer]
        for inner in range(outer):
            value = value - columns[inner] * columns[inner][outer]
        pivot = jnp.sqrt(value[outer])
        columns.append(jnp.where(index >= outer, value / pivot, jnp.zeros_like(value)))
        pivots.append(pivot)
    middle = []
    for outer in range(size):
        accum = -rhs[outer]
        for inner in range(outer):
            accum = accum - columns[inner][outer] * middle[inner]
        middle.append(accum / pivots[outer])
    result = [None] * size
    for outer in range(size - 1, -1, -1):
        accum = middle[outer]
        for inner in range(outer + 1, size):
            accum = accum - columns[outer][inner] * result[inner]
        result[outer] = accum / pivots[outer]
    return jnp.stack(result, 0)


def on_device(state, panel, region, feed_table, step_counts):
    start = state[0, 0]
    row_count = start.shape[1]
    column_count = start.shape[2]
    directions = panel.shape[2]
    tangent = panel[0, 0].reshape(2 * directions, row_count, column_count)
    stacked = jnp.concatenate([start, tangent], 0)
    classes = jnp.arange(feed_table.shape[0], dtype=jnp.int32)
    feed_rate = jnp.sum(
        jnp.where(region[None] == classes[:, None, None], feed_table[:, None, None], 0.0), 0
    )
    step_limit = step_counts[0]
    widened = extended_2(jnp.concatenate([stacked, feed_rate[None]], 0), ((SPACE, 1),), STEPS)
    stacked = widened[:-1]
    feed_wide = widened[-1]
    total_rows = feed_wide.shape[0]
    for step_index in range(STEPS):
        stacked = advance(
            stacked,
            feed_wide[step_index + 1 : total_rows - step_index - 1],
            step_index < step_limit,
        )
    partner_state = swapped(start, "branch", 0)
    arrived = passed_along(stacked, "tm", 1)
    mismatch = (arrived[:2] - start).reshape(-1)
    panel_rows = panel[0, 0].reshape(directions, -1)
    jacobian_panel = arrived[2:].reshape(directions, -1) - panel_rows
    gap = (start - partner_state).reshape(-1)
    total = 2.0 * lax.axis_size("tm") * row_count * lax.axis_size(SPACE) * column_count
    gap_part = jnp.sum(gap * gap)
    along_part = jnp.dot(panel_rows, gap, precision=HIGHEST)
    gap_sum, along_sum = (
        one_axis_at_a_time(gap_part, TM_SPACE),
        one_axis_at_a_time(along_part, TM_SPACE),
    )
    distance = gap_sum / total + SMALL_EPSILON
    deflator = 1.0 / distance + 1.0
    slopes = -2.0 * (along_sum / total) / (distance * distance)
    deflated = deflator * mismatch
    deflated_panel = deflator * jacobian_panel + slopes[:, None] * mismatch[None, :]
    gram_part = jnp.dot(deflated_panel, deflated_panel.T, precision=HIGHEST)
    rhs_part = jnp.dot(deflated_panel, deflated, precision=HIGHEST)
    gram_sum, rhs_sum = (
        one_axis_at_a_time(gram_part, TM_SPACE),
        one_axis_at_a_time(rhs_part, TM_SPACE),
    )
    gram = gram_sum / total
    rhs = rhs_sum / total
    coefficients = solve_small(gram, rhs)
    correction = jnp.dot(coefficients, panel_rows, precision=HIGHEST)
    return (
        deflated.reshape(1, 1, 2, row_count, column_count),
        correction.reshape(1, 1, 2, row_count, column_count),
        coefficients.reshape(1, directions),
    )


def solution(mesh):
    finer = Mesh(
        mesh.devices.reshape(mesh.shape["tm"], 4, 4, mesh.shape["branch"]),
        ("tm", "space_0", "space_1", "branch"),
    )
    in_specs = (
        P("branch", "tm", None, SPACE, None),
        P("branch", "tm", None, None, SPACE, None),
        P(SPACE, None),
        P(),
        P("tm"),
    )
    out_specs = (
        P("branch", "tm", None, SPACE, None),
        P("branch", "tm", None, SPACE, None),
        P("branch", None),
    )
    return jax.shard_map(
        on_device, mesh=finer, in_specs=in_specs, out_specs=out_specs, check_vma=False
    )
```

profile of v0, /device:TPU:2, one launch (start us, length us, event | category | flops | bytes accessed | tf_op | source)
XLA Modules:
  0.0 467.2 jit_solution(3463741294993328432)
XLA Ops:
  0.6 1.0 select_reduce_fusion
  1.6 1.7 pad_maximum_fusion.5
  4.0 1.6 collective-permute-start.1
  6.1 0.8 collective-permute-start.2
  7.6 16.5 %collective-permute-done.1 = f32[35,5,1024]{2,0,1:T(8,128)S(1)} collective-permute-done((f32[35,5,1024]{2,0,1:T(8,128)S(1)}, f32[35,5,1024]{2,0,1:T(8,128)S(1)}, u32[]{:S(2)}, u32[]{:S(2)}) %collective-permute-start.1) | collective-permute-done | bytes 716832 | tf_op jit(solution)/shard_map/ppermute | solution.py:29
  24.5 1.3 collective-permute-done.2
  26.3 0.9 pad_maximum_fusion
  27.2 2.1 fusion.75
  29.5 2.6 fusion.74
  32.2 0.8 add_bitcast_fusion.7
  33.8 0.9 maximum_select_fusion
  34.7 1.8 fusion.87
  36.8 2.0 fusion.86
  38.9 0.8 add_bitcast_fusion.5
  40.6 0.8 maximum_select_fusion.1
  41.5 2.0 fusion.84
  43.7 2.2 fusion.83
  46.0 0.8 add_bitcast_fusion.3
  47.5 0.8 maximum_select_fusion.2
  48.3 1.8 fusion.81
  50.3 2.0 fusion.80
  52.5 0.8 add_bitcast_fusion.1
  54.2 0.9 maximum_select_fusion.3
  55.1 1.3 fusion.78
  56.6 1.8 fusion.77
  58.4 0.7 add_bitcast_fusion.9
  59.6 2.0 maximum_select_fusion.4
  61.6 2.1 collective-permute-start.3
  63.8 1.5 reshape_squeeze.7
  65.3 4.1 copy.58
  70.2 4.1 convolution_bitcast_fusion.1
  74.4 51.4 %all-reduce.1 = (f32[]{:T(128)}, f32[16]{0:T(128)S(1)}) all-reduce(f32[]{:T(128)} %get-tuple-element.31, f32[16]{0:T(128)S(1)} %convolution_bitcast_fusion.1), channel_id=1, replica_groups=mesh['tm'=8,'space_0'=4,'space_1'=4,'branch'=2] {'tm'}, use_global_device_ids=true, to_apply=%region_1.2 | all-reduce | flops 17 | bytes 136 | tf_op jit(solution)/shard_map/psum | solution.py:51
  125.7 11.3 %all-reduce.5 = (f32[]{:T(128)}, f32[16]{0:T(128)S(1)}) all-reduce(f32[]{:T(128)} %get-tuple-element.19, f32[16]{0:T(128)S(1)} %get-tuple-element.20), channel_id=1, replica_groups=mesh['tm'=8,'space_0'=4,'space_1'=4,'branch'=2] {'space_0'}, use_global_device_ids=true, to_apply=%region_2.3 | all-reduce | flops 17 | bytes 136 | tf_op jit(solution)/shard_map/psum | solution.py:51
  137.1 10.6 %all-reduce.3 = (f32[]{:T(128)}, f32[16]{0:T(128)S(1)}) all-reduce(f32[]{:T(128)} %get-tuple-element.27, f32[16]{0:T(128)S(1)} %get-tuple-element.28), channel_id=1, replica_groups=mesh['tm'=8,'space_0'=4,'space_1'=4,'branch'=2] {'space_1'}, use_global_device_ids=true, to_apply=%region_3.4 | all-reduce | flops 17 | bytes 136 | tf_op jit(solution)/shard_map/psum | solution.py:51
  148.6 0.9 broadcast_multiply_fusion
  149.6 3.4 fusion.16
  153.0 1.7 add.356
  154.9 2.9 fusion.105
  157.8 2.6 convolution_bitcast_fusion
  160.4 15.8 %all-reduce = (f32[16]{0:T(128)S(1)}, f32[16,16]{1,0:T(8,128)S(1)}) all-reduce(f32[16]{0:T(128)S(1)} %convolution_bitcast_fusion, f32[16,16]{1,0:T(8,128)S(1)} %fusion.105), channel_id=1, replica_groups=mesh['tm'=8,'space_0'=4,'space_1'=4,'branch'=2] {'tm'}, use_global_device_ids=true, to_apply=%region_8.9 | all-reduce | flops 272 | bytes 2176 | tf_op jit(solution)/shard_map/psum | solution.py:51
  176.2 8.0 %all-reduce.4 = (f32[16]{0:T(128)S(1)}, f32[16,16]{1,0:T(8,128)S(1)}) all-reduce(f32[16]{0:T(128)S(1)} %get-tuple-element.17, f32[16,16]{1,0:T(8,128)S(1)} %get-tuple-element.18), channel_id=1, replica_groups=mesh['tm'=8,'space_0'=4,'space_1'=4,'branch'=2] {'space_0'}, use_global_device_ids=true, to_apply=%region_9.10 | all-reduce | flops 272 | bytes 2176 | tf_op jit(solution)/shard_map/psum | solution.py:51
  184.2 11.2 %all-reduce.2 = (f32[16]{0:T(128)S(1)}, f32[16,16]{1,0:T(8,128)S(1)}) all-reduce(f32[16]{0:T(128)S(1)} %get-tuple-element.25, f32[16,16]{1,0:T(8,128)S(1)} %get-tuple-element.26), channel_id=1, replica_groups=mesh['tm'=8,'space_0'=4,'space_1'=4,'branch'=2] {'space_1'}, use_global_device_ids=true, to_apply=%region_10.11 | all-reduce | flops 272 | bytes 2176 | tf_op jit(solution)/shard_map/psum | solution.py:51
  197.3 0.7 fusion.104
  201.8 4.1 fusion.68
  211.5 5.9 %fusion.59 = (f32[16]{0:T(128)S(1)}, f32[16]{0:T(128)S(1)}, f32[16]{0:T(128)S(1)}, f32[16]{0:T(128)S(1)}, f32[16]{0:T(128)S(1)}, /*index=5*/f32[16]{0:T(128)S(1)}, f32[16]{0:T(128)S(1)}, f32[16]{0:T(128)S(1)}, f32[16]{0:T(128)S(1)}) fusion(f32[16,16]{1,0:T(8,128)S(1)} %broadcast_multiply_fusion.1, f32[]{:T(128)} %bitcast.179, f32[]{:T(128)} %bitcast.163, ...), kind=kLoop, calls=%fused_computation.134 | loop fusion | flops 304 | bytes 1256 | tf_op jit(solution)/shard_map/sub | solution.py:108
  219.3 0.7 fusion.103
  222.0 0.7 fusion.102
  224.6 1.2 multiply_subtract_fusion.12
  226.9 0.7 fusion.101
  230.1 2.0 multiply_subtract_fusion.11
  233.4 0.7 fusion.100
  237.3 2.4 multiply_subtract_fusion.10
  240.9 0.7 fusion.99
  245.5 3.2 multiply_subtract_fusion.9
  255.0 3.7 multiply_subtract_fusion.8
  265.7 4.4 multiply_subtract_fusion.7
  277.7 4.8 %multiply_subtract_fusion.6 = f32[16]{0:T(128)S(1)} fusion(f32[16]{0:T(128)S(1)} %get-tuple-element.9, f32[]{:T(128)} %bitcast.96, f32[]{:T(128)} %bitcast.105, f32[]{:T(128)} %bitcast.104, f32[]{:T(128)} %bitcast.103, f32[]{:T(128)} %bitcast.102, f32[]{:T(128)} %bitcast.101, f32[]{:T(128)} %bitcast.100, f32[]{:T(128)} %bitcast.99, ...), kind=kLoop, calls=%fused_computation.186 | loop fusion | flops 624 | bytes 700 | tf_op jit(solution)/shard_map/sub | solution.py:108
  290.7 5.6 %multiply_subtract_fusion.5 = f32[16]{0:T(128)S(1)} fusion(f32[16]{0:T(128)S(1)} %get-tuple-element.8, f32[]{:T(128)} %bitcast.107, f32[]{:T(128)} %bitcast.117, f32[]{:T(128)} %bitcast.116, f32[]{:T(128)} %bitcast.115, f32[]{:T(128)} %bitcast.114, f32[]{:T(128)} %bitcast.113, f32[]{:T(128)} %bitcast.112, f32[]{:T(128)} %bitcast.111, f32[]{:T(128)} %bitcast.110, ...), kind=kLoop, calls=%fused_computation.185 | loop fusion | flops 704 | bytes 772 | tf_op jit(solution)/shard_map/sub | solution.py:108
  305.0 6.1 %multiply_subtract_fusion.4 = f32[16]{0:T(128)S(1)} fusion(f32[16]{0:T(128)S(1)} %get-tuple-element.7, f32[]{:T(128)} %bitcast.119, f32[]{:T(128)} %bitcast.130, f32[]{:T(128)} %bitcast.129, f32[]{:T(128)} %bitcast.128, f32[]{:T(128)} %bitcast.127, f32[]{:T(128)} %bitcast.126, f32[]{:T(128)} %bitcast.125, f32[]{:T(128)} %bitcast.124, f32[]{:T(128)} %bitcast.123, ...), kind=kLoop, calls=%fused_computation.184 | loop fusion | flops 784 | bytes 844 | tf_op jit(solution)/shard_map/sub | solution.py:108
  320.8 7.2 %multiply_subtract_fusion.3 = f32[16]{0:T(128)S(1)} fusion(f32[16]{0:T(128)S(1)} %get-tuple-element.6, f32[]{:T(128)} %bitcast.132, f32[]{:T(128)} %bitcast.144, f32[]{:T(128)} %bitcast.143, f32[]{:T(128)} %bitcast.142, f32[]{:T(128)} %bitcast.141, f32[]{:T(128)} %bitcast.140, f32[]{:T(128)} %bitcast.139, f32[]{:T(128)} %bitcast.138, f32[]{:T(128)} %bitcast.137, ...), kind=kLoop, calls=%fused_computation.183 | loop fusion | flops 864 | bytes 916 | tf_op jit(solution)/shard_map/sub | solution.py:108
  338.0 7.5 %multiply_subtract_fusion.2 = f32[16]{0:T(128)S(1)} fusion(f32[16]{0:T(128)S(1)} %get-tuple-element.5, f32[]{:T(128)} %bitcast.146, f32[]{:T(128)} %bitcast.159, f32[]{:T(128)} %bitcast.158, f32[]{:T(128)} %bitcast.157, f32[]{:T(128)} %bitcast.156, f32[]{:T(128)} %bitcast.155, f32[]{:T(128)} %bitcast.154, f32[]{:T(128)} %bitcast.153, f32[]{:T(128)} %bitcast.152, ...), kind=kLoop, calls=%fused_computation.182 | loop fusion | flops 944 | bytes 988 | tf_op jit(solution)/shard_map/sub | solution.py:108
  356.6 8.1 %multiply_subtract_fusion.1 = f32[16]{0:T(128)S(1)} fusion(f32[16]{0:T(128)S(1)} %get-tuple-element.4, f32[]{:T(128)} %bitcast.161, f32[]{:T(128)} %bitcast.175, f32[]{:T(128)} %bitcast.174, f32[]{:T(128)} %bitcast.173, f32[]{:T(128)} %bitcast.172, f32[]{:T(128)} %bitcast.171, f32[]{:T(128)} %bitcast.170, f32[]{:T(128)} %bitcast.169, f32[]{:T(128)} %bitcast.168, ...), kind=kLoop, calls=%fused_computation.181 | loop fusion | flops 1024 | bytes 1060 | tf_op jit(solution)/shard_map/sub | solution.py:108
  376.0 8.8 %multiply_subtract_fusion = f32[16]{0:T(128)S(1)} fusion(f32[16]{0:T(128)S(1)} %get-tuple-element.3, f32[]{:T(128)} %bitcast.177, f32[]{:T(128)} %bitcast.192, f32[]{:T(128)} %bitcast.191, f32[]{:T(128)} %bitcast.190, f32[]{:T(128)} %bitcast.189, f32[]{:T(128)} %bitcast.188, f32[]{:T(128)} %bitcast.187, f32[]{:T(128)} %bitcast.186, f32[]{:T(128)} %bitcast.185, ...), kind=kLoop, calls=%fused_computation.180 | loop fusion | flops 1104 | bytes 1132 | tf_op jit(solution)/shard_map/sub | solution.py:108
  464.0 2.2 fusion.17
  (92 shorter events, 26.3 us)
Async XLA Ops:
  4.0 20.1 %collective-permute-start.1 = (f32[35,5,1024]{2,0,1:T(8,128)S(1)}, f32[35,5,1024]{2,0,1:T(8,128)S(1)}, u32[]{:S(2)}, u32[]{:S(2)}) collective-permute-start(f32[35,5,1024]{2,0,1:T(8,128)S(1)} %copy.37), channel_id=1, source_target_pairs={{0,2},{2,4},{4,6},{6,8},{8,10},{10,12},{12,14},{14,16},{16,18},{18... | collective-permute-start | bytes 2150408 | tf_op jit(solution)/shard_map/ppermute | solution.py:29
  6.0 20.3 %copy-start = (f32[1,1,16,2,16,1024]{5,4,3,2,1,0:T(8,128)S(1)}, f32[1,1,16,2,16,1024]{5,4,3,2,1,0:T(8,128)}, u32[]{:S(2)}) copy-start(f32[1,1,16,2,16,1024]{5,4,3,2,1,0:T(8,128)} %param.6) | copy-start | bytes 6291460
  6.0 20.3 %copy-start.1 = (f32[1,1,2,16,1024]{4,3,2,1,0:T(8,128)S(1)}, f32[1,1,2,16,1024]{4,3,2,1,0:T(8,128)}, u32[]{:S(2)}) copy-start(f32[1,1,2,16,1024]{4,3,2,1,0:T(8,128)} %param.5) | copy-start | bytes 393220
  6.1 19.8 %collective-permute-start.2 = (f32[35,5,1024]{2,0,1:T(8,128)S(1)}, f32[35,5,1024]{2,0,1:T(8,128)S(1)}, u32[]{:S(2)}, u32[]{:S(2)}) collective-permute-start(f32[35,5,1024]{2,0,1:T(8,128)S(1)} %copy.38), channel_id=1, source_target_pairs={{2,0},{4,2},{6,4},{8,6},{10,8},{12,10},{14,12},{16,14},{18,16},{20... | collective-permute-start | bytes 2150408 | tf_op jit(solution)/shard_map/ppermute | solution.py:31
  61.6 87.0 %collective-permute-start.3 = (f32[34,16,1024]{2,1,0:T(8,128)}, f32[34,16,1024]{2,1,0:T(8,128)}, u32[]{:S(2)}, u32[]{:S(2)}) collective-permute-start(f32[34,16,1024]{2,1,0:T(8,128)} %maximum_select_fusion.4), channel_id=1, source_target_pairs={{224,0},{0,32},{32,64},{64,96},{96,128},{128,160},{160,192},{192,2... | collective-permute-start | bytes 6684680 | tf_op jit(solution)/shard_map/ppermute | solution.py:47
  63.8 5.7 %collective-permute-start = (f32[2,16,1024]{2,1,0:T(8,128)S(1)}, f32[2,16,1024]{2,1,0:T(8,128)S(1)}, u32[]{:S(2)}, u32[]{:S(2)}) collective-permute-start(f32[2,16,1024]{2,1,0:T(8,128)S(1)} %bitcast.288), channel_id=1, source_target_pairs={{0,1},{1,0},{2,3},{3,2},{4,5},{5,4},{6,7},{7,6},{8,9},{9,8},{10,11... | collective-permute-start | bytes 393224 | tf_op jit(solution)/shard_map/ppermute | solution.py:41
  149.6 5.2 %copy-start.3 = (f32[2,16,1024]{2,1,0:T(8,128)}, f32[2,16,1024]{2,1,0:T(8,128)S(1)}, u32[]{:S(2)}) copy-start(f32[2,16,1024]{2,1,0:T(8,128)S(1)} %get-tuple-element.29) | copy-start | bytes 393220
  160.4 303.5 %copy-start.2 = (f32[2,8,32,1024]{3,2,1,0:T(8,128)S(1)}, f32[2,8,32,1024]{3,2,1,0:T(8,128)}, u32[]{:S(2)}) copy-start(f32[2,8,32,1024]{3,2,1,0:T(8,128)} %copy.58) | copy-start | bytes 6291460
  463.9 3.0 copy-start.4
where the time goes:
time: 476 us; the launch traced here: 467 us
  between operations  175 us (37%)
  blocking collectives  108 us (23%)
  other arithmetic  106 us (22%)
  local copies, waits for them, and re-layouts  43 us (9%)
  waiting for transfers between devices  17.8 us (4%)
  matrix products  11.9 us (2%)
    psum x6, blocking collectives, one_axis_at_a_time(): return functools.reduce(lax.psum, axes, x)  108 us
    sub x16, other arithmetic, solve_small(): value = value - columns[inner] * columns[inner][outer]  75.4 us
    ppermute x1, waiting for transfers between devices, extended_2(): lax.ppermute(tail, axis, [(i, (i + 1) % count) for i in range(count)])  16.5 us
    slice x5, other arithmetic, advance(): interior = extended[:, 1:-1, :]  10.5 us
    slice x10, local copies, waits for them, and re-layouts, laplacian_rows(): jnp.roll(interior, -1, 2)  10.1 us
    slice x16, local copies, waits for them, and re-layouts, solve_small(): pivot = jnp.sqrt(value[outer])  9.57 us
  transfers between devices with their start and end apart: 4, of which 2 were waited for; matrix products, arithmetic and copies ran while one was open for 2% of the time, Pallas kernels for 0%

commit v1 on v0

--- a/solution.py
+++ b/solution.py
@@ -5,6 +5,7 @@
 from jax import lax
 from jax.sharding import Mesh
 from jax.sharding import PartitionSpec as P
+from jax.experimental import pallas as pl
 
 STEPS = 5
 SPACE = ("space_0", "space_1")
@@ -97,31 +98,46 @@
     return jnp.where(active, advanced, interior)
 
 
-def solve_small(gram, rhs):
-    size = gram.shape[0]
-    index = jnp.arange(size)
+def cholesky_kernel(gram_ref, rhs_ref, out_ref):
+    size = gram_ref.shape[0]
+    tile = gram_ref[...]
+    rows = lax.broadcasted_iota(jnp.int32, tile.shape, 0)
+    cols = lax.broadcasted_iota(jnp.int32, tile.shape, 1)
+    diagonal = rows == cols
+    index = rows[:, :1]
     columns = []
     pivots = []
     for outer in range(size):
-        value = gram[:, outer]
-        for inner in range(outer):
-            value = value - columns[inner] * columns[inner][outer]
-        pivot = jnp.sqrt(value[outer])
-        columns.append(jnp.where(index >= outer, value / pivot, jnp.zeros_like(value)))
+        value = jnp.sum(jnp.where(cols == outer, tile, 0.0), axis=1, keepdims=True)
+        pivot = jnp.sqrt(jnp.sum(jnp.where(index == outer, value, 0.0), axis=0, keepdims=True))
+        column = jnp.where(index >= outer, value / pivot, 0.0)
+        row = jnp.sum(jnp.where(diagonal, column, 0.0), axis=0, keepdims=True)
+        tile = tile - column * row
+        columns.append(column)
         pivots.append(pivot)
-    middle = []
+    accum = -jnp.sum(jnp.where(diagonal, rhs_ref[...], 0.0), axis=1, keepdims=True)
+    middle = jnp.zeros_like(accum)
     for outer in range(size):
-        accum = -rhs[outer]
-        for inner in range(outer):
-            accum = accum - columns[inner][outer] * middle[inner]
-        middle.append(accum / pivots[outer])
-    result = [None] * size
+        value = jnp.sum(jnp.where(index == outer, accum, 0.0), axis=0, keepdims=True) / pivots[outer]
+        middle = jnp.where(index == outer, value, middle)
+        accum = accum - columns[outer] * value
+    result = jnp.zeros_like(middle)
     for outer in range(size - 1, -1, -1):
-        accum = middle[outer]
-        for inner in range(outer + 1, size):
-            accum = accum - columns[outer][inner] * result[inner]
-        result[outer] = accum / pivots[outer]
-    return jnp.stack(result, 0)
+        below = jnp.sum(jnp.where(index > outer, columns[outer] * result, 0.0), axis=0, keepdims=True)
+        value = jnp.sum(jnp.where(index == outer, middle, 0.0), axis=0, keepdims=True)
+        result = jnp.where(index == outer, (value - below) / pivots[outer], result)
+    out_ref[...] = jnp.sum(jnp.where(diagonal, result, 0.0), axis=0, keepdims=True)
+
+
+def solve_small(gram, rhs):
+    size = gram.shape[0]
+    lanes = 128
+    padded = jnp.pad(gram, ((0, 0), (0, lanes - size)))
+    rhs_row = jnp.pad(rhs, (0, lanes - size)).reshape(1, lanes)
+    out = pl.pallas_call(
+        cholesky_kernel, out_shape=jax.ShapeDtypeStruct((1, lanes), jnp.float32)
+    )(padded, rhs_row)
+    return out[0, :size]
 
 
 def on_device(state, panel, region, feed_table, step_counts):
@@ -131,11 +147,21 @@
     directions = panel.shape[2]
     tangent = panel[0, 0].reshape(2 * directions, row_count, column_count)
     stacked = jnp.concatenate([start, tangent], 0)
+    following = passed_along(stacked, "tm", -1)
+    partner_state = swapped(start, "branch", 0)
     classes = jnp.arange(feed_table.shape[0], dtype=jnp.int32)
     feed_rate = jnp.sum(
         jnp.where(region[None] == classes[:, None, None], feed_table[:, None, None], 0.0), 0
     )
     step_limit = step_counts[0]
+    panel_rows = panel[0, 0].reshape(directions, -1)
+    gap = (start - partner_state).reshape(-1)
+    total = 2.0 * lax.axis_size("tm") * row_count * lax.axis_size(SPACE) * column_count
+    gap_part = jnp.sum(gap * gap)
+    along_part = jnp.dot(panel_rows, gap, precision=HIGHEST)
+    first_sum = lax.psum(jnp.concatenate([gap_part[None], along_part]), TM_SPACE)
+    gap_sum = first_sum[0]
+    along_sum = first_sum[1:]
     widened = extended_2(jnp.concatenate([stacked, feed_rate[None]], 0), ((SPACE, 1),), STEPS)
     stacked = widened[:-1]
     feed_wide = widened[-1]
@@ -146,32 +172,23 @@
             feed_wide[step_index + 1 : total_rows - step_index - 1],
             step_index < step_limit,
         )
-    partner_state = swapped(start, "branch", 0)
-    arrived = passed_along(stacked, "tm", 1)
-    mismatch = (arrived[:2] - start).reshape(-1)
-    panel_rows = panel[0, 0].reshape(directions, -1)
-    jacobian_panel = arrived[2:].reshape(directions, -1) - panel_rows
-    gap = (start - partner_state).reshape(-1)
-    total = 2.0 * lax.axis_size("tm") * row_count * lax.axis_size(SPACE) * column_count
-    gap_part = jnp.sum(gap * gap)
-    along_part = jnp.dot(panel_rows, gap, precision=HIGHEST)
-    gap_sum, along_sum = (
-        one_axis_at_a_time(gap_part, TM_SPACE),
-        one_axis_at_a_time(along_part, TM_SPACE),
-    )
+    arrived = passed_along(stacked[:2], "tm", 1)
+    mismatch = (arrived - start).reshape(-1)
+    next_mismatch = (stacked[:2] - following[:2]).reshape(-1)
+    next_jacobian = stacked[2:].reshape(directions, -1) - following[2:].reshape(directions, -1)
     distance = gap_sum / total + SMALL_EPSILON
     deflator = 1.0 / distance + 1.0
     slopes = -2.0 * (along_sum / total) / (distance * distance)
     deflated = deflator * mismatch
-    deflated_panel = deflator * jacobian_panel + slopes[:, None] * mismatch[None, :]
+    next_deflated = deflator * next_mismatch
+    deflated_panel = deflator * next_jacobian + slopes[:, None] * next_mismatch[None, :]
     gram_part = jnp.dot(deflated_panel, deflated_panel.T, precision=HIGHEST)
-    rhs_part = jnp.dot(deflated_panel, deflated, precision=HIGHEST)
-    gram_sum, rhs_sum = (
-        one_axis_at_a_time(gram_part, TM_SPACE),
-        one_axis_at_a_time(rhs_part, TM_SPACE),
-    )
-    gram = gram_sum / total
-    rhs = rhs_sum / total
+    rhs_part = jnp.dot(deflated_panel, next_deflated, precision=HIGHEST)
+    second_sum = lax.psum(
+        jnp.concatenate([gram_part.reshape(-1), rhs_part]), TM_SPACE
+    )
+    gram = second_sum[: directions * directions].reshape(directions, directions) / total
+    rhs = second_sum[directions * directions :] / total
     coefficients = solve_small(gram, rhs)
     correction = jnp.dot(coefficients, panel_rows, precision=HIGHEST)
     return (

time: 476 us -> 814 us (1.71)
  blocking collectives: 108 us -> 722 us
  between operations: 175 us -> 2.31 us
  other arithmetic: 106 us -> 31.9 us
  waiting for transfers between devices: 17.8 us -> 0.01 us
  local copies, waits for them, and re-layouts: 43 us -> 27.1 us
    psum x6 -> x2, blocking collectives: 108 us -> 722 us  [the longest x1 372 us: on_device(): lax.psum(jnp.concatenate([gap_part[None], along_part]), TM_SPACE)]
    sub x16 -> x0, other arithmetic: 75.4 us -> none  [solve_small(): value = value - columns[inner] * columns[inner][outer]]
    slice x32 -> x0, local copies, waits for them, and re-layouts: 20.4 us -> none  [the longest x16 9.57 us: solve_small(): pivot = jnp.sqrt(value[outer])]
    ppermute x1, waiting for transfers between devices: 16.5 us -> 0.01 us  [extended_2(): lax.ppermute(tail, axis, [(i, (i + 1) % count) for i in range(count)])]
  transfers between devices with their start and end apart: 4 -> 5, of which waited for: 2 -> 0; matrix products, arithmetic and copies ran while one was open for 2% -> 7% of each run, Pallas kernels for 0% -> 0%
where the time goes in v1:
time: 814 us; the launch traced here: 808 us
  blocking collectives  722 us (89%)
  other arithmetic  31.9 us (4%)
  local copies, waits for them, and re-layouts  27.1 us (3%)
  matrix products  13.4 us (2%)
  starting transfers between devices  8.33 us (1%)
    psum x1, blocking collectives, on_device(): lax.psum(jnp.concatenate([gap_part[None], along_part]), TM_SPACE)  372 us
    psum x1, blocking collectives, on_device(): lax.psum(jnp.concatenate([gram_part.reshape(-1), rhs_part]), TM_SPACE)  350 us
  transfers between devices with their start and end apart: 5, of which 0 were waited for; matrix products, arithmetic and copies ran while one was open for 7% of the time, Pallas kernels for 0%

profile of v1, /device:TPU:2, one launch (start us, length us, event | category | flops | bytes accessed | tf_op | source)
XLA Modules:
  0.0 808.0 jit_solution(11361416359294530595)
XLA Ops:
  0.7 1.0 select_reduce_fusion
  1.7 1.7 pad_maximum_fusion.5
  3.5 0.3 fusion.75
  3.8 0.4 copy.35
  4.3 1.6 collective-permute-start.1
  5.8 1.4 copy.36
  7.2 0.8 collective-permute-start.2
  8.0 1.6 pad_maximum_fusion.6
  9.6 5.6 collective-permute-start.4
  15.2 1.6 reshape_squeeze.6
  17.5 4.2 copy.56
  21.7 0.6 multiply_reduce_fusion
  22.5 4.1 convolution_bitcast_fusion.1
  26.6 0.7 pad_maximum_fusion.11
  27.4 372.0 %psum.14 = f32[17]{0:T(128)S(1)} all-reduce(f32[17]{0:T(128)S(1)} %pad_maximum_fusion.11), channel_id=1, replica_groups=mesh['tm'=8,'space_0'=4,'space_1'=4,'branch'=2] {'tm','space_0','space_1'}, use_global_device_ids=true, to_apply=%region_1.2 | all-reduce | flops 17 | bytes 136 | tf_op jit(solution)/shard_map/psum | solution.py:162
  399.7 1.6 copy.37
  401.3 1.6 copy.38
  402.9 0.9 pad_maximum_fusion
  403.7 2.1 fusion.61
  405.8 0.2 fusion.62
  406.0 2.0 fusion.60
  408.2 0.8 add_bitcast_fusion.7
  409.1 0.4 pad_maximum_fusion.1
  409.4 0.4 copy.39
  409.8 0.9 maximum_select_fusion
  410.8 1.8 fusion.73
  412.6 0.2 fusion.74
  412.8 2.2 fusion.72
  415.1 0.8 add_bitcast_fusion.5
  415.9 0.5 pad_maximum_fusion.2
  416.5 0.4 copy.50
  416.9 0.8 maximum_select_fusion.1
  417.7 2.0 fusion.70
  419.7 0.2 fusion.71
  419.9 2.0 fusion.69
  422.1 0.8 add_bitcast_fusion.3
  422.9 0.3 pad_maximum_fusion.3
  423.2 0.4 copy.51
  423.6 0.8 maximum_select_fusion.2
  424.4 1.8 fusion.67
  426.2 0.2 fusion.68
  426.4 2.3 fusion.66
  428.8 0.8 add_bitcast_fusion.1
  429.6 0.4 pad_maximum_fusion.4
  430.0 0.4 copy.52
  430.4 0.9 maximum_select_fusion.3
  431.3 0.2 fusion.65
  431.4 1.3 fusion.64
  432.8 1.8 fusion.63
  434.6 0.5 add_bitcast_fusion.9
  435.4 0.6 maximum_select_fusion.4
  436.1 0.9 broadcast_multiply_fusion
  437.0 3.4 fusion.16
  440.4 1.7 add.345
  442.3 2.9 fusion.76
  445.2 2.6 convolution_bitcast_fusion
  447.9 349.8 %psum.15 = f32[272]{0:T(512)S(1)} all-reduce(f32[272]{0:T(512)S(1)} %pad_maximum_fusion.10), channel_id=1, replica_groups=mesh['tm'=8,'space_0'=4,'space_1'=4,'branch'=2] {'tm','space_0','space_1'}, use_global_device_ids=true, to_apply=%region_3.4 | all-reduce | flops 272 | bytes 2176 | tf_op jit(solution)/shard_map/psum | solution.py:187
  797.9 0.5 pad_bitcast_fusion.rhs_ref
  798.4 0.3 collective-permute-start.3
  798.7 0.6 pad.8.gram_ref
  799.3 3.1 shard_map.76
  802.4 3.8 fusion.17
  806.1 0.7 copy.60
  806.8 0.7 multiply_bitcast_fusion
  (28 shorter events, 1.6 us)
Async XLA Ops:
  0.6 21.1 %collective-permute-start = (f32[2,16,1024]{2,1,0:T(8,128)}, f32[2,16,1024]{2,1,0:T(8,128)S(1)}, u32[]{:S(2)}, u32[]{:S(2)}) collective-permute-start(f32[2,16,1024]{2,1,0:T(8,128)} %bitcast.122), channel_id=1, source_target_pairs={{0,1},{1,0},{2,3},{3,2},{4,5},{5,4},{6,7},{7,6},{8,9},{9,8},{10,11... | collective-permute-start | bytes 393224 | tf_op jit(solution)/shard_map/ppermute | solution.py:42
  3.8 4.2 copy-start
  3.8 4.2 copy-start.1
  4.3 395.4 %collective-permute-start.1 = (f32[35,5,1024]{2,0,1:T(8,128)S(1)}, f32[35,5,1024]{2,0,1:T(8,128)}, u32[]{:S(2)}, u32[]{:S(2)}) collective-permute-start(f32[35,5,1024]{2,0,1:T(8,128)S(1)} %copy.35), channel_id=1, source_target_pairs={{0,2},{2,4},{4,6},{6,8},{8,10},{10,12},{12,14},{14,16},{16,18},{18... | collective-permute-start | bytes 2150408 | tf_op jit(solution)/shard_map/ppermute | solution.py:30
  7.2 394.0 %collective-permute-start.2 = (f32[35,5,1024]{2,0,1:T(8,128)}, f32[35,5,1024]{2,0,1:T(8,128)}, u32[]{:S(2)}, u32[]{:S(2)}) collective-permute-start(f32[35,5,1024]{2,0,1:T(8,128)} %copy.36), channel_id=1, source_target_pairs={{2,0},{4,2},{6,4},{8,6},{10,8},{12,10},{14,12},{16,14},{18,16},{20... | collective-permute-start | bytes 2150408 | tf_op jit(solution)/shard_map/ppermute | solution.py:32
  9.6 426.4 %collective-permute-start.4 = (f32[34,16,1024]{2,1,0:T(8,128)}, f32[34,16,1024]{2,1,0:T(8,128)}, u32[]{:S(2)}, u32[]{:S(2)}) collective-permute-start(f32[34,16,1024]{2,1,0:T(8,128)} %pad_maximum_fusion.6), channel_id=1, source_target_pairs={{32,0},{64,32},{96,64},{128,96},{160,128},{192,160},{224,192},{0,2... | collective-permute-start | bytes 6684680 | tf_op jit(solution)/shard_map/ppermute | solution.py:48
  798.4 8.5 %collective-permute-start.3 = (f32[2,16,1024]{2,1,0:T(8,128)S(1)}, f32[2,16,1024]{2,1,0:T(8,128)S(1)}, u32[]{:S(2)}, u32[]{:S(2)}) collective-permute-start(f32[2,16,1024]{2,1,0:T(8,128)S(1)} %get-tuple-element.72), channel_id=1, source_target_pairs={{224,0},{0,32},{32,64},{64,96},{96,128},{128,160},{160,192},{192,2... | collective-permute-start | bytes 393224 | tf_op jit(solution)/shard_map/ppermute | solution.py:48
